TPU v7x, 256 devices: a whole 4x4x8 slice. The times are simulated.
256 devices in a mesh: dp: 64 (over z, y, core), fsdp: 4 (over x).
Axes of the slice: x: 4, y: 4, z: 8, core: 2. Of those that a mesh axis runs over, the one named last changes fastest.
Arguments:
- feats: bfloat16 [64, 4, 8, 128, 256], P('dp', 'fsdp'), may hold values from -6 to 6
- grad_out: bfloat16 [64, 4, 8, 128, 256], P('dp', 'fsdp'), may hold values from -6 to 6
- kernel: bfloat16 [27, 256, 256], P(None, 'fsdp'), may hold values from -0.25 to 0.25
- send_bricks: int32 [64, 4, 64, 2], P('dp', 'fsdp'), may hold values from -1 to 7, as said below
- kmap: int32 [64, 4, 27, 2, 3], P('dp', 'fsdp'), may hold values from 0 to 135, as said below
- pair_count: int32 [64, 4, 27], P('dp', 'fsdp'), may hold values from 1 to 3, as said below
Outputs:
- out_feats: bfloat16 [64, 4, 8, 128, 256], P('dp', 'fsdp')
- in_grad: bfloat16 [64, 4, 8, 128, 256], P('dp', 'fsdp')
- kernel_grad: float32 [27, 256, 256], P(None, 'fsdp')
Inputs may be any that keep to these rules, and one draw needn't show every extreme that they name: `send_bricks`: entry (d, f, p, c) names the brick of device (d, f) sent to device (p, f) in slot c, or -1 for an empty slot. A device sends nothing to itself, fills exactly 48 slots, and fills both slots of at least one peer. kmap[d, f, t, 0, s] is an input brick of pool[d, f]: below 8 an own brick, else received slot p * 2 + c after the 8 own ones, and then always a slot that its sender filled. kmap[d, f, t, 1, s] is an output brick, below 8. Slots that are not live hold such ids too. `pair_count`: on some device every offset has 3 live slots.
All inputs are finite; a program needn't handle non-finite values.
Results may differ from a plain program's by a relative error of at most 0.0046.
Values may be sent and summed in bfloat16 or wider, within the bound.
No kernel may reach another device: no remote copies, remote signals or barrier semaphores. Data moves between devices by JAX's collectives and lax.ppermute only.
A program may use at most 192 MiB of HBM per device.

v0:
```python
import jax
import jax.numpy as jnp
from jax import lax
from jax.sharding import PartitionSpec as P


def on_device(feats, grad_out, kernel, send_bricks, kmap, pair_count):
    own_rows = feats[0, 0]
    upstream_rows = grad_out[0, 0]
    senders = send_bricks[0, 0]
    peer_total = senders.shape[0]
    slot_cap = senders.shape[1]
    brick_total = own_rows.shape[0]
    brick_rows = own_rows.shape[1]
    channels = own_rows.shape[2]
    filled = senders >= 0
    outgoing = own_rows[jnp.maximum(senders, 0)] * filled[:, :, None, None].astype(jnp.bfloat16)
    incoming = lax.all_to_all(outgoing, "dp", split_axis=0, concat_axis=0, tiled=True)
    weights = lax.all_gather(kernel, "fsdp", axis=1, tiled=True)
    pool = jnp.concatenate(
        [own_rows, incoming.reshape(peer_total * slot_cap, brick_rows, channels)], axis=0
    )
    pool_total = pool.shape[0]
    source_map = kmap[0, 0, :, 0, :]
    target_map = kmap[0, 0, :, 1, :]
    counts = pair_count[0, 0]
    tap_total = source_map.shape[0]
    slot_total = source_map.shape[1]
    active = (jnp.arange(slot_total)[None, :] < counts[:, None]).astype(jnp.bfloat16)
    inputs = pool[source_map] * active[:, :, None, None]
    upstream = upstream_rows[target_map] * active[:, :, None, None]
    contrib = jnp.einsum("tsvc,tcd->tsvd", inputs, weights, preferred_element_type=jnp.float32)
    produced = jax.ops.segment_sum(
        contrib.reshape(tap_total * slot_total, brick_rows, channels),
        target_map.reshape(-1),
        num_segments=brick_total,
    )
    backward = jnp.einsum("tsvd,tcd->tsvc", upstream, weights, preferred_element_type=jnp.float32)
    pool_grad = jax.ops.segment_sum(
        backward.reshape(tap_total * slot_total, brick_rows, channels),
        source_map.reshape(-1),
        num_segments=pool_total,
    )
    partial_value = jnp.einsum(
        "tsvc,tsvd->tcd", inputs, upstream, preferred_element_type=jnp.float32
    )
    ghosts = (
        pool_grad[brick_total:]
        .astype(jnp.bfloat16)
        .reshape(peer_total, slot_cap, brick_rows, channels)
    )
    returned = lax.all_to_all(ghosts, "dp", split_axis=0, concat_axis=0, tiled=True)
    owners = jnp.where(filled, senders, brick_total).reshape(-1)
    gathered_back = jax.ops.segment_sum(
        returned.reshape(peer_total * slot_cap, brick_rows, channels).astype(jnp.float32),
        owners,
        num_segments=brick_total + 1,
    )[:brick_total]
    in_grad = (pool_grad[:brick_total] + gathered_back).astype(jnp.bfloat16)
    divisor = jnp.float32(4 * lax.axis_size("dp") * lax.axis_size("fsdp"))
    shard_width = kernel.shape[1]
    summed = lax.psum(partial_value, ("dp", "fsdp"))
    portion = lax.dynamic_slice_in_dim(summed, lax.axis_index("fsdp") * shard_width, shard_width, 1)
    kernel_grad = portion / divisor
    return (produced.astype(jnp.bfloat16)[None, None], in_grad[None, None], kernel_grad)


def solution(mesh):
    placed = (
        P("dp", "fsdp", None, None, None),
        P("dp", "fsdp", None, None, None),
        P(None, "fsdp", None),
        P("dp", "fsdp", None, None),
        P("dp", "fsdp", None, None, None),
        P("dp", "fsdp", None),
    )
    return jax.shard_map(
        on_device,
        mesh=mesh,
        in_specs=placed,
        out_specs=(
            P("dp", "fsdp", None, None, None),
            P("dp", "fsdp", None, None, None),
            P(None, "fsdp", None),
        ),
        check_vma=False,
    )
```

profile of v0, /device:TPU:2, one launch (start us, length us, event | category | flops | bytes accessed | tf_op | source)
XLA Modules:
  0.0 672.3 jit_solution(8817993394391642369)
XLA Ops:
  8.0 0.0 copy-start
  8.0 0.7 fusion.20
  8.8 0.7 broadcast_maximum_fusion
  9.4 0.1 copy.22
  9.5 0.1 copy.21
  9.6 0.1 reshape.152
  9.8 7.5 %gather_fusion = bf16[128,128,256]{2,1,0:T(8,128)(2,1)} fusion(bf16[8,128,256]{2,1,0:T(8,128)(2,1)} %bitcast.48, s32[1024]{0:T(1024)S(1)} %pad_clamp_fusion.2), kind=kCustom, calls=%fused_computation | custom fusion | bytes 16777728 | tf_op jit(solution)/shard_map/gather | solution.py:17
  17.3 7.3 %broadcast_multiply_fusion = bf16[64,2,128,256]{3,2,1,0:T(8,128)(2,1)} fusion(bf16[64,2,128,256]{3,2,1,0:T(8,128)(2,1)} %bitcast.52, bf16[64,2]{1,0:T(8,128)(2,1)S(1)} %copy.22), kind=kLoop, calls=%fused_computation.16 | loop fusion | flops 4194304 | bytes 16777472 | tf_op jit(solution)/shard_map/mul | solution.py:17
  24.6 12.5 %all-to-all-start = ((bf16[64,2,128,256]{3,2,1,0:T(8,128)(2,1)}), bf16[64,2,128,256]{3,2,1,0:T(8,128)(2,1)}, u32[]{:S(2)}, u32[]{:S(2)}) async-start(bf16[64,2,128,256]{3,2,1,0:T(8,128)(2,1)} %broadcast_multiply_fusion), calls=%async_computation | async-start | bytes 16777216 | tf_op jit(solution)/shard_map/all_to_all | solution.py:18
  37.1 0.0 all-gather.2.cloned.1.call-start
  37.1 0.7 all-gather.2.cloned.1.call-update
  37.8 0.1 copy.27
  37.9 0.1 reshape.168
  38.0 0.1 copy.26
  38.1 0.1 reshape.184
  38.3 5.6 gather_fusion.2
  43.9 8.0 %copy.28 = bf16[27,3,128,256]{2,3,1,0:T(8,128)(2,1)} copy(bf16[27,3,128,256]{3,2,1,0:T(8,128)(2,1)} %bitcast.55) | data formatting | bytes 10616832 | tf_op jit(solution)/shard_map/gather | solution.py:31
  51.9 0.1 fusion.19
  52.0 33.4 %all-gather.2.cloned.1.call-done = bf16[27,256,256]{2,1,0:T(8,128)(2,1)} async-done(((bf16[27,64,256]{2,1,0:T(8,128)(2,1)}), bf16[27,256,256]{2,1,0:T(8,128)(2,1)}) %all-gather.2.cloned.1.call-update) | async-done | bytes 3538960 | tf_op jit(solution)/shard_map/all_gather | solution.py:19
  85.4 9.4 %fusion.2 = f32[27,3,128,256]{3,2,1,0:T(8,128)} fusion(bf16[27,3,128,256]{2,3,1,0:T(8,128)(2,1)} %copy.28, bf16[27,256,256]{2,1,0:T(8,128)(2,1)} %all-gather.2.cloned.1.call-done, bf16[27,3]{1,0:T(8,128)(2,1)S(1)} %fusion.19), kind=kOutput, calls=%fused_computation.11 | convolution fusion | flops 1361608704 | bytes 19464354 | tf_op jit(solution)/shard_map/tsvd,tcd->tsvc/dot_general | solution.py:38
  94.8 8.4 %broadcast_in_dim.26 = f32[136,128,256]{2,1,0:T(8,128)} broadcast(f32[]{:T(128)} %constant.8.clone.1), dimensions={} | broadcast | bytes 17825796 | tf_op jit(solution)/shard_map/broadcast_in_dim | solution.py:39
  103.1 28.6 %scatter_fusion.1 = f32[136,128,256]{2,1,0:T(8,128)} fusion(f32[136,128,256]{2,1,0:T(8,128)} %broadcast_in_dim.26, s32[81]{0:T(128)S(1)} %reshape.184, f32[81,128,256]{2,1,0:T(8,128)} %bitcast.51), kind=kCustom, calls=%fused_computation.4 | custom fusion | flops 2654208 | bytes 31850820 | tf_op jit(solution)/shard_map/scatter-add | solution.py:39
  131.7 9.0 %slice.41 = bf16[128,128,256]{2,1,0:T(8,128)(2,1)} slice(f32[136,128,256]{2,1,0:T(8,128)} %scatter_fusion.1), slice={[8:136], [0:128], [0:256]} | slice | bytes 16777216 | tf_op jit(solution)/shard_map/slice | solution.py:48
  140.7 82.6 %all-to-all-done = bf16[64,2,128,256]{3,2,1,0:T(8,128)(2,1)} async-done(((bf16[64,2,128,256]{3,2,1,0:T(8,128)(2,1)}), bf16[64,2,128,256]{3,2,1,0:T(8,128)(2,1)}, u32[]{:S(2)}, u32[]{:S(2)}) %all-to-all-start) | async-done | bytes 8388640 | tf_op jit(solution)/shard_map/all_to_all | solution.py:18
  223.2 6.5 all-to-all-start.1
  229.8 0.2 all-reduce.2.cloned.1.call-start
  230.0 0.1 copy.23
  230.1 0.1 reshape.160
  230.2 7.6 %pad_maximum_fusion = bf16[136,128,256]{2,1,0:T(8,128)(2,1)} fusion(bf16[128,128,256]{2,1,0:T(8,128)(2,1)} %bitcast.3, bf16[8,128,256]{2,1,0:T(8,128)(2,1)S(1)} %bitcast.49), kind=kLoop, calls=%fused_computation.7 | loop fusion | flops 4456448 | bytes 17825792 | tf_op jit(solution)/shard_map/concatenate | solution.py:20
  237.9 9.2 %gather_fusion.1 = bf16[81,128,256]{2,1,0:T(8,128)(2,1)} fusion(bf16[136,128,256]{2,1,0:T(8,128)(2,1)} %pad_maximum_fusion, s32[1024]{0:T(1024)S(1)} %pad_clamp_fusion.1), kind=kCustom, calls=%fused_computation.1 | custom fusion | bytes 10617156 | tf_op jit(solution)/shard_map/gather | solution.py:30
  247.0 8.0 %copy.24 = bf16[27,3,128,256]{2,3,1,0:T(8,128)(2,1)} copy(bf16[27,3,128,256]{3,2,1,0:T(8,128)(2,1)} %bitcast.54) | data formatting | bytes 10616832 | tf_op jit(solution)/shard_map/gather | solution.py:30
  255.1 9.0 %fusion.9 = f32[27,256,256]{2,1,0:T(8,128)} fusion(bf16[27,3,128,256]{2,3,1,0:T(8,128)(2,1)} %copy.28, bf16[27,3,128,256]{2,3,1,0:T(8,128)(2,1)} %copy.24, bf16[27,3]{1,0:T(8,128)(2,1)S(1)} %fusion.19), kind=kOutput, calls=%fused_computation.19 | convolution fusion | flops 1364262912 | bytes 17694882 | tf_op jit(solution)/shard_map/tsvc,tsvd->tcd/dot_general | solution.py:44
  264.1 0.0 all-reduce.2.cloned.1.call-update
  264.1 0.6 copy-done.4
  264.8 0.1 copy.30
  264.9 0.1 copy.20
  265.0 0.1 reshape.176
  265.1 0.1 squeeze.19
  265.2 9.4 %fusion.5 = f32[27,3,128,256]{3,2,1,0:T(8,128)} fusion(bf16[27,3,128,256]{2,3,1,0:T(8,128)(2,1)} %copy.24, bf16[27,256,256]{2,1,0:T(8,128)(2,1)} %all-gather.2.cloned.1.call-done, bf16[27,3]{1,0:T(8,128)(2,1)S(1)} %fusion.19), kind=kOutput, calls=%fused_computation.14 | convolution fusion | flops 1361608704 | bytes 19464354 | tf_op jit(solution)/shard_map/tsvc,tcd->tsvd/dot_general | solution.py:32
  274.6 0.1 broadcast_in_dim.12
  274.7 18.1 %scatter_fusion = f32[8,128,256]{2,1,0:T(8,128)S(1)} fusion(f32[8,128,256]{2,1,0:T(8,128)S(1)} %broadcast_in_dim.12, s32[81]{0:T(128)S(1)} %reshape.176, f32[81,128,256]{2,1,0:T(8,128)} %bitcast.50), kind=kCustom, calls=%fused_computation.3 | custom fusion | flops 2654208 | bytes 31850820 | tf_op jit(solution)/shard_map/scatter-add | solution.py:33
  292.7 0.8 convert_bitcast_fusion
  293.6 330.5 %all-reduce.2.cloned.1.call-done = f32[27,256,256]{2,1,0:T(8,128)} async-done(((f32[27,256,256]{2,1,0:T(8,128)}), f32[27,256,256]{2,1,0:T(8,128)}) %all-reduce.2.cloned.1.call-update) | async-done | bytes 7077904 | tf_op jit(solution)/shard_map/psum | solution.py:62
  624.1 2.9 dynamic-slice_multiply_fusion
  627.0 11.5 %bitcast_convert_fusion = f32[128,128,256]{2,1,0:T(8,128)} fusion(bf16[64,2,128,256]{3,2,1,0:T(8,128)(2,1)} %all-to-all-done.1), kind=kLoop, calls=%fused_computation.8 | loop fusion | flops 4194304 | bytes 25165824 | tf_op jit(solution)/shard_map/convert_element_type | solution.py:55
  638.5 0.1 broadcast_in_dim.27
  638.6 24.1 %scatter_fusion.2 = f32[9,128,256]{2,1,0:T(8,128)S(1)} fusion(f32[9,128,256]{2,1,0:T(8,128)S(1)} %broadcast_in_dim.27, s32[128]{0:T(128)S(1)} %fusion.21, f32[128,128,256]{2,1,0:T(8,128)} %bitcast_convert_fusion), kind=kCustom, calls=%fused_computation.5 | custom fusion | flops 4194304 | bytes 50332160 | tf_op jit(solution)/shard_map/scatter-add | solution.py:54
  662.7 2.1 fusion.18
  (17 shorter events, 0.1 us)
Async XLA Ops:
  8.0 30.3 %copy-start = (bf16[1,1,8,128,256]{4,3,2,1,0:T(8,128)(2,1)S(1)}, bf16[1,1,8,128,256]{4,3,2,1,0:T(8,128)(2,1)}, u32[]{:S(2)}) copy-start(bf16[1,1,8,128,256]{4,3,2,1,0:T(8,128)(2,1)} %param.7) | copy-start | bytes 1572868
  24.6 13.2 %copy-start.3 = (s32[1,1,27,2,3]{2,3,4,1,0:T(2,128)S(1)}, s32[1,1,27,2,3]{2,3,4,1,0:T(2,128)}, u32[]{:S(2)}) copy-start(s32[1,1,27,2,3]{2,3,4,1,0:T(2,128)} %param.10) | copy-start | bytes 1948
  24.6 198.7 %all-to-all-start = ((bf16[64,2,128,256]{3,2,1,0:T(8,128)(2,1)}), bf16[64,2,128,256]{3,2,1,0:T(8,128)(2,1)}, u32[]{:S(2)}, u32[]{:S(2)}) async-start(bf16[64,2,128,256]{3,2,1,0:T(8,128)(2,1)} %broadcast_multiply_fusion), calls=%async_computation | async-start | bytes 16777216 | tf_op jit(solution)/shard_map/all_to_all | solution.py:18
  37.1 48.3 %all-gather.2.cloned.1.call-start = ((), (), s32[]{:S(2)}) async-start(), calls=%async_computation.2 | async-start | bytes 4423680 | tf_op jit(solution)/shard_map/all_gather | solution.py:19
  43.9 8.0 %copy-start.5 = (s32[1,1,27]{2,1,0:T(1,128)S(1)}, s32[1,1,27]{2,1,0:T(1,128)}, u32[]{:S(2)}) copy-start(s32[1,1,27]{2,1,0:T(1,128)} %param.11) | copy-start | bytes 328
  223.2 7.0 %copy-start.2 = (bf16[1,1,8,128,256]{4,3,2,1,0:T(8,128)(2,1)S(1)}, bf16[1,1,8,128,256]{4,3,2,1,0:T(8,128)(2,1)}, u32[]{:S(2)}) copy-start(bf16[1,1,8,128,256]{4,3,2,1,0:T(8,128)(2,1)} %param.6) | copy-start | bytes 1572868
  223.2 403.7 %all-to-all-start.1 = ((bf16[64,2,128,256]{3,2,1,0:T(8,128)(2,1)}), bf16[64,2,128,256]{3,2,1,0:T(8,128)(2,1)}, u32[]{:S(2)}, u32[]{:S(2)}) async-start(bf16[64,2,128,256]{3,2,1,0:T(8,128)(2,1)} %bitcast.53), calls=%async_computation.1 | async-start | bytes 16777216 | tf_op jit(solution)/shard_map/all_to_all | solution.py:52
  229.8 394.3 %all-reduce.2.cloned.1.call-start = ((), (), s32[]{:S(2)}) async-start(), calls=%async_computation.3 | async-start | bytes 14155776 | tf_op jit(solution)/shard_map/psum | solution.py:62
  264.1 0.7 copy-start.4
  638.6 26.3 %copy-start.1 = (bf16[1,1,8,128,256]{4,3,2,1,0:T(8,128)(2,1)S(1)}, bf16[1,1,8,128,256]{4,3,2,1,0:T(8,128)(2,1)}, u32[]{:S(2)}) copy-start(bf16[1,1,8,128,256]{4,3,2,1,0:T(8,128)(2,1)} %param.7) | copy-start | bytes 1572868
Sparse Core Ops, SparseCore 0:
  39.7 45.6 all-gather.1
Sparse Core Ops, SparseCore 1:
  264.2 359.9 all-reduce.1
where the time goes:
time: 674 us; the launch traced here: 672 us
  waiting for transfers between devices  447 us (66%)
  other arithmetic  105 us (16%)
  local copies, waits for them, and re-layouts  57.9 us (9%)
  matrix products  27.7 us (4%)
  starting transfers between devices  19.3 us (3%)
  between operations  15.6 us (2%)
    psum x1, waiting for transfers between devices, on_device(): summed = lax.psum(partial_value, ('dp', 'fsdp'))  331 us
    all_to_all x1, waiting for transfers between devices, on_device(): lax.all_to_all(outgoing, 'dp', split_axis=0, concat_axis=0, tiled=True)  82.6 us
    all_gather x1, waiting for transfers between devices, on_device(): weights = lax.all_gather(kernel, 'fsdp', axis=1, tiled=True)  33.4 us
    scatter-add x1, other arithmetic, on_device(): jax.ops.segment_sum(backward.reshape(tap_total * slot_total, brick_rows,...  28.6 us
    scatter-add x1, other arithmetic, on_device(): jax.ops.segment_sum(returned.reshape(peer_total * slot_cap, brick_rows, c...  24.1 us
    scatter-add x1, other arithmetic, on_device(): jax.ops.segment_sum(contrib.reshape(tap_total * slot_total, brick_rows, c...  18.1 us
    gather x2, local copies, waits for them, and re-layouts, on_device(): inputs = pool[source_map] * active[:, :, None, None]  17.2 us
    gather x2, local copies, waits for them, and re-layouts, on_device(): upstream = upstream_rows[target_map] * active[:, :, None, None]  13.6 us
  transfers between devices with their start and end apart: 4, of which 3 were waited for; matrix products, arithmetic and copies ran while one was open for 20% of the time, Pallas kernels for 0%

commit v1 on v0

--- a/solution.py
+++ b/solution.py
@@ -16,7 +16,32 @@
     filled = senders >= 0
     outgoing = own_rows[jnp.maximum(senders, 0)] * filled[:, :, None, None].astype(jnp.bfloat16)
     incoming = lax.all_to_all(outgoing, "dp", split_axis=0, concat_axis=0, tiled=True)
-    weights = lax.all_gather(kernel, "fsdp", axis=1, tiled=True)
+    work_now = lax.axis_size("fsdp")
+    small = lax.axis_index("fsdp")
+    current_arr, taken_in, block_now = (work_now, small, kernel.shape[1])
+    row_list = [ii * current_arr if src_i == 1 else ii for src_i, ii in enumerate(kernel.shape)]
+    weights = lax.dynamic_update_slice_in_dim(
+        jnp.zeros(row_list, kernel.dtype), kernel, taken_in * block_now, axis=1
+    )
+    top = then = kernel
+    for dev in range(1, current_arr // 2 + 1):
+        top = lax.ppermute(
+            top,
+            axis_name="fsdp",
+            perm=[(src_i, (src_i + 1) % current_arr) for src_i in range(current_arr)],
+        )
+        weights = lax.dynamic_update_slice_in_dim(
+            weights, top, (taken_in - dev) % current_arr * block_now, axis=1
+        )
+        if 2 * dev < current_arr:
+            then = lax.ppermute(
+                then,
+                axis_name="fsdp",
+                perm=[(src_i, (src_i - 1) % current_arr) for src_i in range(current_arr)],
+            )
+            weights = lax.dynamic_update_slice_in_dim(
+                weights, then, (taken_in + dev) % current_arr * block_now, axis=1
+            )
     pool = jnp.concatenate(
         [own_rows, incoming.reshape(peer_total * slot_cap, brick_rows, channels)], axis=0
     )

time: 674 us -> 634 us (0.941)
  waiting for transfers between devices: 447 us -> 407 us
    psum x1, waiting for transfers between devices: 331 us -> 152 us  [on_device(): summed = lax.psum(partial_value, ('dp', 'fsdp'))]
    all_to_all x1, waiting for transfers between devices: 0.01 us -> 141 us  [on_device(): lax.all_to_all(ghosts, 'dp', split_axis=0, concat_axis=0, tiled=True)]
    all_gather x1 -> x0, waiting for transfers between devices: 33.4 us -> none  [on_device(): weights = lax.all_gather(kernel, 'fsdp', axis=1, tiled=True)]
    ppermute x0 -> x3, waiting for transfers between devices: none -> 23.8 us  [the longest x2 23.8 us: on_device(): lax.ppermute(top, axis_name='fsdp', perm=[(src_i, (src_i + 1) % current_a...]
    all_to_all x1, waiting for transfers between devices: 82.6 us -> 91 us  [on_device(): lax.all_to_all(outgoing, 'dp', split_axis=0, concat_axis=0, tiled=True)]
  transfers between devices with their start and end apart: 4 -> 6, of which waited for: 3 -> 5; matrix products, arithmetic and copies ran while one was open for 20% -> 27% of each run, Pallas kernels for 0% -> 0%
where the time goes in v1:
time: 634 us; the launch traced here: 633 us
  waiting for transfers between devices  407 us (64%)
  other arithmetic  104 us (16%)
  local copies, waits for them, and re-layouts  59.9 us (9%)
  matrix products  24.3 us (4%)
  starting transfers between devices  22.9 us (4%)
  between operations  14.3 us (2%)
    psum x1, waiting for transfers between devices, on_device(): summed = lax.psum(partial_value, ('dp', 'fsdp'))  152 us
    all_to_all x1, waiting for transfers between devices, on_device(): lax.all_to_all(ghosts, 'dp', split_axis=0, concat_axis=0, tiled=True)  141 us
    all_to_all x1, waiting for transfers between devices, on_device(): lax.all_to_all(outgoing, 'dp', split_axis=0, concat_axis=0, tiled=True)  91 us
    scatter-add x1, other arithmetic, on_device(): jax.ops.segment_sum(backward.reshape(tap_total * slot_total, brick_rows,...  28.3 us
    scatter-add x1, other arithmetic, on_device(): jax.ops.segment_sum(returned.reshape(peer_total * slot_cap, brick_rows, c...  24.1 us
    ppermute x2, waiting for transfers between devices, on_device(): lax.ppermute(top, axis_name='fsdp', perm=[(src_i, (src_i + 1) % current_a...  23.8 us
    scatter-add x1, other arithmetic, on_device(): jax.ops.segment_sum(contrib.reshape(tap_total * slot_total, brick_rows, c...  18.1 us
    gather x2, local copies, waits for them, and re-layouts, on_device(): inputs = pool[source_map] * active[:, :, None, None]  17.2 us
  transfers between devices with their start and end apart: 6, of which 5 were waited for; matrix products, arithmetic and copies ran while one was open for 27% of the time, Pallas kernels for 0%

profile of v1, /device:TPU:2, one launch (start us, length us, event | category | flops | bytes accessed | tf_op | source)
XLA Modules:
  0.0 632.8 jit_solution(10473587570004183911)
XLA Ops:
  7.2 0.7 fusion.20
  7.9 0.7 broadcast_maximum_fusion
  8.6 0.1 copy.22
  8.8 0.1 reshape.152
  9.0 7.5 %gather_fusion = bf16[128,128,256]{2,1,0:T(8,128)(2,1)} fusion(bf16[8,128,256]{2,1,0:T(8,128)(2,1)} %bitcast.48, s32[1024]{0:T(1024)S(1)} %pad_clamp_fusion.2), kind=kCustom, calls=%fused_computation | custom fusion | bytes 16777728 | tf_op jit(solution)/shard_map/gather | solution.py:17
  16.4 7.3 %broadcast_multiply_fusion = bf16[64,2,128,256]{3,2,1,0:T(8,128)(2,1)} fusion(bf16[64,2,128,256]{3,2,1,0:T(8,128)(2,1)} %bitcast.52, bf16[64,2]{1,0:T(8,128)(2,1)S(1)} %copy.22), kind=kLoop, calls=%fused_computation.16 | loop fusion | flops 4194304 | bytes 16777472 | tf_op jit(solution)/shard_map/mul | solution.py:17
  23.7 12.5 %all-to-all-start = ((bf16[64,2,128,256]{3,2,1,0:T(8,128)(2,1)}), bf16[64,2,128,256]{3,2,1,0:T(8,128)(2,1)}, u32[]{:S(2)}, u32[]{:S(2)}) async-start(bf16[64,2,128,256]{3,2,1,0:T(8,128)(2,1)} %broadcast_multiply_fusion), calls=%async_computation | async-start | bytes 16777216 | tf_op jit(solution)/shard_map/all_to_all | solution.py:18
  36.2 1.6 collective-permute-start
  37.8 0.5 collective-permute-start.1
  38.4 0.1 copy.27
  38.5 0.1 reshape.168
  38.6 19.2 %collective-permute-done = bf16[27,64,256]{2,1,0:T(8,128)(2,1)S(1)} collective-permute-done((bf16[27,64,256]{2,1,0:T(8,128)(2,1)S(1)}, bf16[27,64,256]{2,1,0:T(8,128)(2,1)S(1)}, u32[]{:S(2)}, u32[]{:S(2)}) %collective-permute-start) | collective-permute-done | bytes 884768 | tf_op jit(solution)/shard_map/ppermute | solution.py:28
  57.8 1.5 collective-permute-start.2
  59.4 0.1 copy.26
  59.6 5.6 gather_fusion.2
  65.2 8.0 %copy.28 = bf16[27,3,128,256]{2,3,1,0:T(8,128)(2,1)} copy(bf16[27,3,128,256]{3,2,1,0:T(8,128)(2,1)} %bitcast.55) | data formatting | bytes 10616832 | tf_op jit(solution)/shard_map/gather | solution.py:56
  73.2 0.4 broadcast_in_dim.28
  73.6 0.1 constant_dynamic-update-slice_fusion.3
  73.7 0.1 copy-done.8
  73.9 0.1 constant_dynamic-update-slice_fusion.2
  74.0 0.1 constant_dynamic-update-slice_fusion.1
  74.1 4.6 collective-permute-done.2
  78.7 1.2 constant_dynamic-update-slice_fusion
  80.0 5.8 fusion.2
  85.8 8.3 %broadcast_in_dim.30 = f32[136,128,256]{2,1,0:T(8,128)} broadcast(f32[]{:T(128)} %constant.20.clone.1), dimensions={} | broadcast | bytes 17825796 | tf_op jit(solution)/shard_map/broadcast_in_dim | solution.py:64
  94.1 28.3 %scatter_fusion.1 = f32[136,128,256]{2,1,0:T(8,128)} fusion(f32[136,128,256]{2,1,0:T(8,128)} %broadcast_in_dim.30, s32[81]{0:T(128)S(1)} %reshape.184, f32[81,128,256]{2,1,0:T(8,128)} %bitcast.51), kind=kCustom, calls=%fused_computation.4 | custom fusion | flops 2654208 | bytes 31850820 | tf_op jit(solution)/shard_map/scatter-add | solution.py:64
  122.4 9.0 %slice.41 = bf16[128,128,256]{2,1,0:T(8,128)(2,1)} slice(f32[136,128,256]{2,1,0:T(8,128)} %scatter_fusion.1), slice={[8:136], [0:128], [0:256]} | slice | bytes 16777216 | tf_op jit(solution)/shard_map/slice | solution.py:73
  131.4 91.0 %all-to-all-done = bf16[64,2,128,256]{3,2,1,0:T(8,128)(2,1)} async-done(((bf16[64,2,128,256]{3,2,1,0:T(8,128)(2,1)}), bf16[64,2,128,256]{3,2,1,0:T(8,128)(2,1)}, u32[]{:S(2)}, u32[]{:S(2)}) %all-to-all-start) | async-done | bytes 8388640 | tf_op jit(solution)/shard_map/all_to_all | solution.py:18
  222.4 6.5 %all-to-all-start.1 = ((bf16[64,2,128,256]{3,2,1,0:T(8,128)(2,1)}), bf16[64,2,128,256]{3,2,1,0:T(8,128)(2,1)}, u32[]{:S(2)}, u32[]{:S(2)}) async-start(bf16[64,2,128,256]{3,2,1,0:T(8,128)(2,1)} %bitcast.53), calls=%async_computation.1 | async-start | bytes 16777216 | tf_op jit(solution)/shard_map/all_to_all | solution.py:77
  228.9 0.3 all-reduce.2.cloned.1.call-start
  229.2 0.1 copy.23
  229.3 0.1 reshape.160
  229.4 7.6 %pad_maximum_fusion = bf16[136,128,256]{2,1,0:T(8,128)(2,1)} fusion(bf16[128,128,256]{2,1,0:T(8,128)(2,1)} %bitcast.3, bf16[8,128,256]{2,1,0:T(8,128)(2,1)S(1)} %bitcast.49), kind=kLoop, calls=%fused_computation.7 | loop fusion | flops 4456448 | bytes 17825792 | tf_op jit(solution)/shard_map/concatenate | solution.py:45
  237.0 9.2 %gather_fusion.1 = bf16[81,128,256]{2,1,0:T(8,128)(2,1)} fusion(bf16[136,128,256]{2,1,0:T(8,128)(2,1)} %pad_maximum_fusion, s32[1024]{0:T(1024)S(1)} %pad_clamp_fusion.1), kind=kCustom, calls=%fused_computation.1 | custom fusion | bytes 10617156 | tf_op jit(solution)/shard_map/gather | solution.py:55
  246.2 8.0 %copy.24 = bf16[27,3,128,256]{2,3,1,0:T(8,128)(2,1)} copy(bf16[27,3,128,256]{3,2,1,0:T(8,128)(2,1)} %bitcast.54) | data formatting | bytes 10616832 | tf_op jit(solution)/shard_map/gather | solution.py:55
  254.3 9.1 %fusion.9 = f32[27,256,256]{2,1,0:T(8,128)} fusion(bf16[27,3,128,256]{2,3,1,0:T(8,128)(2,1)} %copy.28, bf16[27,3,128,256]{2,3,1,0:T(8,128)(2,1)} %copy.24, bf16[27,3]{1,0:T(8,128)(2,1)S(1)} %fusion.19), kind=kOutput, calls=%fused_computation.19 | convolution fusion | flops 1364262912 | bytes 17694882 | tf_op jit(solution)/shard_map/tsvc,tsvd->tcd/dot_general | solution.py:69
  263.4 0.7 copy-done.7
  264.2 0.1 copy.20
  264.4 0.1 squeeze.19
  264.5 9.4 %fusion.5 = f32[27,3,128,256]{3,2,1,0:T(8,128)} fusion(bf16[27,3,128,256]{2,3,1,0:T(8,128)(2,1)} %copy.24, bf16[27,256,256]{2,1,0:T(8,128)(2,1)} %copy-done.3, bf16[27,3]{1,0:T(8,128)(2,1)S(1)} %fusion.19), kind=kOutput, calls=%fused_computation.14 | convolution fusion | flops 1361608704 | bytes 19464354 | tf_op jit(solution)/shard_map/tsvc,tcd->tsvd/dot_general | solution.py:57
  274.0 18.1 %scatter_fusion = f32[8,128,256]{2,1,0:T(8,128)S(1)} fusion(f32[8,128,256]{2,1,0:T(8,128)S(1)} %broadcast_in_dim.14, s32[81]{0:T(128)S(1)} %reshape.176, f32[81,128,256]{2,1,0:T(8,128)} %bitcast.50), kind=kCustom, calls=%fused_computation.3 | custom fusion | flops 2654208 | bytes 31850820 | tf_op jit(solution)/shard_map/scatter-add | solution.py:58
  292.0 0.8 convert_bitcast_fusion
  292.9 140.7 %all-to-all-done.1 = bf16[64,2,128,256]{3,2,1,0:T(8,128)(2,1)} async-done(((bf16[64,2,128,256]{3,2,1,0:T(8,128)(2,1)}), bf16[64,2,128,256]{3,2,1,0:T(8,128)(2,1)}, u32[]{:S(2)}, u32[]{:S(2)}) %all-to-all-start.1) | async-done | bytes 8388640 | tf_op jit(solution)/shard_map/all_to_all | solution.py:77
  433.6 11.5 %bitcast_convert_fusion = f32[128,128,256]{2,1,0:T(8,128)} fusion(bf16[64,2,128,256]{3,2,1,0:T(8,128)(2,1)} %all-to-all-done.1), kind=kLoop, calls=%fused_computation.8 | loop fusion | flops 4194304 | bytes 25165824 | tf_op jit(solution)/shard_map/convert_element_type | solution.py:80
  445.3 24.1 %scatter_fusion.2 = f32[9,128,256]{2,1,0:T(8,128)S(1)} fusion(f32[9,128,256]{2,1,0:T(8,128)S(1)} %broadcast_in_dim.31, s32[128]{0:T(128)S(1)} %fusion.21, f32[128,128,256]{2,1,0:T(8,128)} %bitcast_convert_fusion), kind=kCustom, calls=%fused_computation.5 | custom fusion | flops 4194304 | bytes 50332160 | tf_op jit(solution)/shard_map/scatter-add | solution.py:79
  469.4 2.1 fusion.18
  471.6 151.5 %all-reduce.2.cloned.1.call-done = f32[27,256,256]{2,1,0:T(8,128)} async-done(((f32[27,256,256]{2,1,0:T(8,128)}), f32[27,256,256]{2,1,0:T(8,128)}) %all-reduce.2.cloned.1.call-update) | async-done | bytes 7077904 | tf_op jit(solution)/shard_map/psum | solution.py:87
  623.1 2.9 dynamic-slice_multiply_fusion
  (31 shorter events, 0.7 us)
Async XLA Ops:
  7.2 52.4 %copy-start = (bf16[1,1,8,128,256]{4,3,2,1,0:T(8,128)(2,1)S(1)}, bf16[1,1,8,128,256]{4,3,2,1,0:T(8,128)(2,1)}, u32[]{:S(2)}) copy-start(bf16[1,1,8,128,256]{4,3,2,1,0:T(8,128)(2,1)} %param.7) | copy-start | bytes 1572868
  23.7 12.5 %copy-start.5 = (bf16[27,64,256]{2,1,0:T(8,128)(2,1)S(1)}, bf16[27,64,256]{2,1,0:T(8,128)(2,1)}, u32[]{:S(2)}) copy-start(bf16[27,64,256]{2,1,0:T(8,128)(2,1)} %param.8) | copy-start | bytes 2654212
  23.7 14.6 %copy-start.6 = (s32[1,1,27,2,3]{2,3,4,1,0:T(2,128)S(1)}, s32[1,1,27,2,3]{2,3,4,1,0:T(2,128)}, u32[]{:S(2)}) copy-start(s32[1,1,27,2,3]{2,3,4,1,0:T(2,128)} %param.10) | copy-start | bytes 1948
  23.7 198.7 %all-to-all-start = ((bf16[64,2,128,256]{3,2,1,0:T(8,128)(2,1)}), bf16[64,2,128,256]{3,2,1,0:T(8,128)(2,1)}, u32[]{:S(2)}, u32[]{:S(2)}) async-start(bf16[64,2,128,256]{3,2,1,0:T(8,128)(2,1)} %broadcast_multiply_fusion), calls=%async_computation | async-start | bytes 16777216 | tf_op jit(solution)/shard_map/all_to_all | solution.py:18
  36.2 21.6 %collective-permute-start = (bf16[27,64,256]{2,1,0:T(8,128)(2,1)S(1)}, bf16[27,64,256]{2,1,0:T(8,128)(2,1)S(1)}, u32[]{:S(2)}, u32[]{:S(2)}) collective-permute-start(bf16[27,64,256]{2,1,0:T(8,128)(2,1)S(1)} %copy-done.5), channel_id=1, source_target_pairs={{0,1},{1,2},{2,3},{3,0},{4,5},{5,6},{6,7},{7,4},{8,9},{9,10},{10,1... | collective-permute-start | bytes 2654216 | tf_op jit(solution)/shard_map/ppermute | solution.py:28
  37.8 36.2 %collective-permute-start.1 = (bf16[27,64,256]{2,1,0:T(8,128)(2,1)S(1)}, bf16[27,64,256]{2,1,0:T(8,128)(2,1)S(1)}, u32[]{:S(2)}, u32[]{:S(2)}) collective-permute-start(bf16[27,64,256]{2,1,0:T(8,128)(2,1)S(1)} %copy-done.5), channel_id=1, source_target_pairs={{0,3},{1,0},{2,1},{3,2},{4,7},{5,4},{6,5},{7,6},{8,11},{9,8},{10,9... | collective-permute-start | bytes 2654216 | tf_op jit(solution)/shard_map/ppermute | solution.py:37
  57.8 20.9 %collective-permute-start.2 = (bf16[27,64,256]{2,1,0:T(8,128)(2,1)S(1)}, bf16[27,64,256]{2,1,0:T(8,128)(2,1)}, u32[]{:S(2)}, u32[]{:S(2)}) collective-permute-start(bf16[27,64,256]{2,1,0:T(8,128)(2,1)S(1)} %collective-permute-done), channel_id=1, source_target_pairs={{0,1},{1,2},{2,3},{3,0},{4,5},{5,6},{6,7},{7,4},{8,9},{9,10},{10,1... | collective-permute-start | bytes 2654216 | tf_op jit(solution)/shard_map/ppermute | solution.py:28
  73.2 0.7 copy-start.8
  73.2 6.8 %copy-start.4 = (bf16[27,3,128,256]{2,3,1,0:T(8,128)(2,1)S(1)}, bf16[27,3,128,256]{2,3,1,0:T(8,128)(2,1)}, u32[]{:S(2)}) copy-start(bf16[27,3,128,256]{2,3,1,0:T(8,128)(2,1)} %copy.28) | copy-start | bytes 15925252
  80.0 5.8 copy-start.3
  222.4 7.0 %copy-start.2 = (bf16[1,1,8,128,256]{4,3,2,1,0:T(8,128)(2,1)S(1)}, bf16[1,1,8,128,256]{4,3,2,1,0:T(8,128)(2,1)}, u32[]{:S(2)}) copy-start(bf16[1,1,8,128,256]{4,3,2,1,0:T(8,128)(2,1)} %param.6) | copy-start | bytes 1572868
  222.4 211.2 %all-to-all-start.1 = ((bf16[64,2,128,256]{3,2,1,0:T(8,128)(2,1)}), bf16[64,2,128,256]{3,2,1,0:T(8,128)(2,1)}, u32[]{:S(2)}, u32[]{:S(2)}) async-start(bf16[64,2,128,256]{3,2,1,0:T(8,128)(2,1)} %bitcast.53), calls=%async_computation.1 | async-start | bytes 16777216 | tf_op jit(solution)/shard_map/all_to_all | solution.py:77
  228.9 394.2 %all-reduce.2.cloned.1.call-start = ((), (), s32[]{:S(2)}) async-start(), calls=%async_computation.2 | async-start | bytes 14155776 | tf_op jit(solution)/shard_map/psum | solution.py:87
  263.4 0.7 copy-start.7
  445.3 180.7 %copy-start.1 = (bf16[1,1,8,128,256]{4,3,2,1,0:T(8,128)(2,1)S(1)}, bf16[1,1,8,128,256]{4,3,2,1,0:T(8,128)(2,1)}, u32[]{:S(2)}) copy-start(bf16[1,1,8,128,256]{4,3,2,1,0:T(8,128)(2,1)} %param.7) | copy-start | bytes 1572868
Sparse Core Ops, SparseCore 0:
  263.5 359.4 all-reduce.1
